TPU v7x, 128 devices: a whole 4x4x4 slice. The times are simulated.
128 devices in a mesh: dom: 16 (over x, z_hi, core), cls: 8 (over z_lo, y).
Axes of the slice: x: 4, y: 4, z: 4 (z_hi: 2, z_lo: 2; z = z_hi * 2 + z_lo), core: 2. Of those that a mesh axis runs over, the one named last changes fastest.
Arguments:
- particles: bfloat16 [2048, 16384], P(('dom', 'cls')), may hold values from -6 to 6
- averages: float32 [256, 16384], P('cls'), may hold values from -4 to 4
- prior_mass: float32 [256], P('cls'), may hold values from 1 to 8
- group_ids: int32 [4, 2048, 1], P(None, ('dom', 'cls')), may hold values from 0 to 7; in each aligned block of 16 rows (0 to 15, 16 to 31, ..., all dimensions but the last counted through in order) at most 6 rows name the same one
- class_ids: int32 [4, 2048], P(None, ('dom', 'cls')), may hold values from 0 to 31
- rot_ids: int32 [4, 2048], P(None, ('dom', 'cls')), may hold values from 0 to 63
- weights: bfloat16 [4, 2048], P(None, ('dom', 'cls')), may hold values from 0.25 to 4
- owners: int32 [4], replicated, may hold values from 0 to 7
Outputs:
- scores: float32 [4, 2048, 2048], P(None, ('dom', 'cls'))
- final_averages: float32 [256, 16384], P('cls')
Inputs may be any that keep to these rules, and one draw needn't show every extreme that they name: `group_ids`: in every step, at most 6 of the 16 particles of one device name one class group; in every step some device's particles reach 6 for some group.
All inputs are finite; a program needn't handle non-finite values.
Results may differ from a plain program's by a relative error of at most 0.0027.
Values may be sent and summed in bfloat16 or wider, within the bound.
No kernel may reach another device: no remote copies, remote signals or barrier semaphores. Data moves between devices by JAX's collectives and lax.ppermute only.
A program may use at most 256 MiB of HBM per device.

v0:
```python
import math
import jax
import jax.numpy as jnp
from jax import lax
from jax.sharding import PartitionSpec as P

RADII = 128
ANGLES = 128
ROT = 64
STEPS = 4
ASTEP = 2


def rotate_each(cube, shifts):
    src = jnp.arange(ANGLES, dtype=jnp.int32)
    dst = (src[None, :, None] + shifts[:, None, None]) % ANGLES
    perm = (dst == src[None, None, :]).astype(cube.dtype)
    out = jnp.einsum("iab,ibc->iac", cube, perm, preferred_element_type=jnp.float32)
    return out.astype(cube.dtype)


def per_device(particles, averages, prior_mass, group_ids, class_ids, rot_ids, weights, owners):
    per_dev = particles.shape[0]
    pixels = particles.shape[1]
    groups = lax.axis_size("cls")
    doms = lax.axis_size("dom")
    chunk = pixels // doms
    per_group = averages.shape[0]
    capacity = per_dev * 3 // 8
    slots = groups * capacity
    me_dom = lax.axis_index("dom")
    me_cls = lax.axis_index("cls")
    cube = particles.reshape(per_dev, RADII, ANGLES)
    doubled = jnp.concatenate([cube, cube], axis=2)
    scale = 1.0 / math.sqrt(pixels)
    turns_block = min(ROT, max(8, 512 // per_dev))
    block_starts = list(range(0, ROT, turns_block))
    send_img = []
    send_wts = []
    for step in range(STEPS):
        shifts = rot_ids[step] * ASTEP
        rotated = rotate_each(cube, shifts).reshape(per_dev, pixels)
        target = group_ids[step, :, 0]
        onehot_group = (target[:, None] == jnp.arange(groups, dtype=jnp.int32)[None, :]).astype(
            jnp.int32
        )
        rank = jnp.sum((jnp.cumsum(onehot_group, axis=0) - 1) * onehot_group, axis=1)
        slot_of = target * capacity + rank
        placing = (slot_of[None, :] == jnp.arange(slots, dtype=jnp.int32)[:, None]).astype(
            jnp.bfloat16
        )
        images = jnp.dot(placing, rotated, preferred_element_type=jnp.float32).astype(jnp.bfloat16)
        images = images.reshape(groups, capacity, doms, chunk).transpose(2, 0, 1, 3)
        send_img.append(images)
        class_hot = (
            class_ids[step][:, None] == jnp.arange(per_group, dtype=jnp.int32)[None, :]
        ).astype(jnp.bfloat16)
        weighted_hot = class_hot * weights[step][:, None]
        wts = jnp.dot(placing, weighted_hot, preferred_element_type=jnp.float32).astype(
            jnp.bfloat16
        )
        wts = jnp.broadcast_to(
            wts.reshape(1, groups, capacity, per_group), (doms, groups, capacity, per_group)
        )
        send_wts.append(wts)
    send_img = jnp.stack(send_img, axis=2).reshape(doms * groups, STEPS, capacity, chunk)
    send_wts = jnp.stack(send_wts, axis=2).reshape(doms * groups, STEPS, capacity, per_group)
    got_img = lax.all_to_all(send_img, ("dom", "cls"), 0, 0, tiled=True)
    got_wts = lax.all_to_all(send_wts, ("dom", "cls"), 0, 0, tiled=True)
    totals = lax.dot_general(
        got_wts, got_img, (((0, 2), (0, 2)), ((1,), (1,))), preferred_element_type=jnp.float32
    )
    mass = jnp.sum(got_wts.astype(jnp.float32), axis=(0, 2))
    current = lax.dynamic_slice_in_dim(averages, me_dom * chunk, chunk, axis=1)
    ref_chunks = []
    for step in range(STEPS):
        current = (prior_mass[:, None] * current + totals[step]) / (prior_mass + mass[step])[
            :, None
        ]
        piece = current.astype(jnp.bfloat16)
        piece = jnp.where(me_cls == owners[step], piece, jnp.zeros_like(piece))
        ref_chunks.append(piece)
    ref_chunks = lax.psum(jnp.stack(ref_chunks, axis=0), "cls")
    all_refs = lax.all_gather(ref_chunks, "dom", axis=0, tiled=False)
    all_refs = all_refs.transpose(1, 2, 0, 3).reshape(STEPS, per_group, pixels)
    final = lax.all_gather(current, "dom", axis=0, tiled=False)
    final = final.transpose(1, 0, 2).reshape(per_group, pixels)
    all_scores = []
    for step in range(STEPS):
        refs = all_refs[step]
        pieces = []
        for first in block_starts:
            count = min(turns_block, ROT - first)
            views = [
                doubled[:, :, ANGLES - turn * ASTEP : 2 * ANGLES - turn * ASTEP]
                for turn in range(first, first + count)
            ]
            rolled = jnp.stack(views, axis=1).reshape(per_dev * count, pixels)
            product = lax.dot_general(
                rolled, refs, (((1,), (1,)), ((), ())), preferred_element_type=jnp.float32
            )
            pieces.append(product.reshape(per_dev, count * per_group))
        stacked = jnp.concatenate(pieces, axis=1)
        all_scores.append(stacked * scale)
    return (jnp.stack(all_scores, axis=0), final)


def solution(mesh):
    return jax.shard_map(
        per_device,
        mesh=mesh,
        in_specs=(
            P(("dom", "cls"), None),
            P("cls", None),
            P("cls"),
            P(None, ("dom", "cls"), None),
            P(None, ("dom", "cls")),
            P(None, ("dom", "cls")),
            P(None, ("dom", "cls")),
            P(),
        ),
        out_specs=(P(None, ("dom", "cls"), None), P("cls", None)),
        check_vma=False,
    )
```

profile of v0, /device:TPU:1, one launch (start us, length us, event | category | flops | bytes accessed | tf_op | source)
XLA Modules:
  0.0 466.9 jit_solution(8276902115353094044)
XLA Ops:
  14.4 1.3 reshape.477
  15.7 11.7 %all-to-all-start = ((bf16[128,2,384]{2,1,0:T(2,128)(2,1)}), bf16[128,2,384]{2,1,0:T(2,128)(2,1)S(1)}, u32[]{:S(2)}, u32[]{:S(2)}) async-start(bf16[128,2,384]{2,1,0:T(2,128)(2,1)} %reshape.477), calls=%async_computation | async-start | bytes 393216 | tf_op jit(solution)/shard_map/all_to_all | solution.py:69
  28.2 1.1 copy.284
  41.1 1.3 copy.363
  42.4 3.2 pad_maximum_fusion
  45.6 10.3 %copy.227 = bf16[128,4,6,1024]{3,1,2,0:T(4,128)(2,1)} copy(bf16[128,4,6,1024]{3,0,2,1:T(8,128)(2,1)} %pad_maximum_fusion) | data formatting | bytes 12582912 | tf_op jit(solution)/shard_map/stack | solution.py:66
  55.9 10.2 %all-to-all-start.1 = ((bf16[128,4,6,1024]{3,1,2,0:T(4,128)(2,1)}), bf16[128,4,6,1024]{3,1,2,0:T(4,128)(2,1)}, u32[]{:S(2)}, u32[]{:S(2)}) async-start(bf16[128,4,6,1024]{3,1,2,0:T(4,128)(2,1)} %copy.227), calls=%async_computation.1 | async-start | bytes 12582912 | tf_op jit(solution)/shard_map/all_to_all | solution.py:68
  72.5 1.1 fusion.103
  85.1 60.6 %all-to-all-done.1 = bf16[128,4,6,1024]{3,1,2,0:T(4,128)(2,1)} async-done(((bf16[128,4,6,1024]{3,1,2,0:T(4,128)(2,1)}), bf16[128,4,6,1024]{3,1,2,0:T(4,128)(2,1)}, u32[]{:S(2)}, u32[]{:S(2)}) %all-to-all-start.1) | async-done | bytes 6291488 | tf_op jit(solution)/shard_map/all_to_all | solution.py:68
  145.6 9.7 %fusion.30 = f32[4,32,1024]{2,1,0:T(8,128)S(1)} fusion(bf16[128,4,6,1024]{3,1,2,0:T(4,128)(2,1)} %all-to-all-done.1, bf16[128,4,6,32]{3,1,2,0:T(4,128)(2,1)S(1)} %bitcast.549), kind=kOutput, calls=%fused_computation.44 | convolution fusion | flops 201326592 | bytes 7012352 | tf_op jit(solution)/shard_map/dot_general | solution.py:70
  175.8 1.1 fusion.75
  176.9 51.4 %all-reduce.2.cloned.1.call-done = bf16[1,4,32,1024]{3,2,1,0:T(8,128)(2,1)} async-done(((bf16[1,4,32,1024]{3,2,1,0:T(8,128)(2,1)}), bf16[1,4,32,1024]{3,2,1,0:T(8,128)(2,1)}) %all-reduce.2.cloned.1.call-update) | async-done | bytes 262160 | tf_op jit(solution)/shard_map/psum | solution.py:83
  229.3 14.2 %copy.209 = bf16[16,32,128,128]{3,2,1,0:T(8,128)(2,1)} copy(bf16[16,32,128,128]{3,2,0,1:T(8,128)(2,1)} %fusion.74) | data formatting | bytes 33554432 | tf_op jit(solution)/shard_map/stack | solution.py:98
  275.3 3.2 copy.283
  278.4 10.8 %all-gather.4.cloned.1.call-done = bf16[16,4,32,1024]{3,2,1,0:T(8,128)(2,1)} async-done(((bf16[1,4,32,1024]{3,2,1,0:T(8,128)(2,1)}), bf16[16,4,32,1024]{3,2,1,0:T(8,128)(2,1)}) %all-gather.4.cloned.1.call-update) | async-done | bytes 4194320 | tf_op jit(solution)/shard_map/all_gather | solution.py:84
  289.2 2.6 fusion.172
  292.0 1.2 copy.298
  293.3 18.1 %fusion = f32[512,32]{1,0:T(8,128)} fusion(bf16[32,16384]{1,0:T(8,128)(2,1)S(1)} %bitcast.574, bf16[64,8,128,128]{3,2,1,0:T(8,128)(2,1)} %bitcast.216), kind=kOutput, calls=%fused_computation.4 | convolution fusion | flops 536870912 | bytes 17891328 | tf_op jit(solution)/shard_map/dot_general | solution.py:99
  311.4 24.1 %fusion.2 = f32[512,32]{1,0:T(8,128)} fusion(bf16[32,16384]{1,0:T(8,128)(2,1)} %bitcast.576, bf16[64,8,128,128]{3,2,1,0:T(8,128)(2,1)} %bitcast.216), kind=kOutput, calls=%fused_computation.6 | convolution fusion | flops 536870912 | bytes 17891328 | tf_op jit(solution)/shard_map/dot_general | solution.py:99
  335.5 18.4 %fusion.8 = f32[512,32]{1,0:T(8,128)S(1)} fusion(bf16[32,16384]{1,0:T(8,128)(2,1)} %bitcast.575, bf16[64,8,128,128]{3,2,1,0:T(8,128)(2,1)S(1)} %bitcast.545), kind=kOutput, calls=%fused_computation.12 | convolution fusion | flops 536870912 | bytes 17891328 | tf_op jit(solution)/shard_map/dot_general | solution.py:99
  353.9 18.8 %fusion.10 = f32[512,32]{1,0:T(8,128)S(1)} fusion(bf16[32,16384]{1,0:T(8,128)(2,1)} %bitcast.577, bf16[64,8,128,128]{3,2,1,0:T(8,128)(2,1)S(1)} %bitcast.546), kind=kOutput, calls=%fused_computation.14 | convolution fusion | flops 536870912 | bytes 17891328 | tf_op jit(solution)/shard_map/dot_general | solution.py:99
  372.7 1.1 copy.297
  373.7 23.9 %fusion.4 = f32[512,32]{1,0:T(8,128)} fusion(bf16[32,16384]{1,0:T(8,128)(2,1)} %bitcast.580, bf16[64,8,128,128]{3,2,1,0:T(8,128)(2,1)} %bitcast.216), kind=kOutput, calls=%fused_computation.8 | convolution fusion | flops 536870912 | bytes 17891328 | tf_op jit(solution)/shard_map/dot_general | solution.py:99
  397.7 18.2 %fusion.12 = f32[512,32]{1,0:T(8,128)} fusion(bf16[32,16384]{1,0:T(8,128)(2,1)S(1)} %bitcast.581, bf16[64,8,128,128]{3,2,1,0:T(8,128)(2,1)S(1)} %bitcast.547), kind=kOutput, calls=%fused_computation.16 | convolution fusion | flops 536870912 | bytes 17891328 | tf_op jit(solution)/shard_map/dot_general | solution.py:99
  416.0 17.6 %fusion.6 = f32[512,32]{1,0:T(8,128)} fusion(bf16[32,16384]{1,0:T(8,128)(2,1)S(1)} %bitcast.578, bf16[64,8,128,128]{3,2,1,0:T(8,128)(2,1)} %bitcast.216), kind=kOutput, calls=%fused_computation.10 | convolution fusion | flops 536870912 | bytes 17891328 | tf_op jit(solution)/shard_map/dot_general | solution.py:99
  433.6 17.9 %fusion.14 = f32[512,32]{1,0:T(8,128)} fusion(bf16[32,16384]{1,0:T(8,128)(2,1)S(1)} %bitcast.579, bf16[64,8,128,128]{3,2,1,0:T(8,128)(2,1)S(1)} %bitcast.548), kind=kOutput, calls=%fused_computation.18 | convolution fusion | flops 536870912 | bytes 17891328 | tf_op jit(solution)/shard_map/dot_general | solution.py:99
  451.5 1.1 concatenate.71
  452.6 1.1 concatenate.68
  453.7 1.1 concatenate.62
  454.7 1.1 concatenate.65
  455.8 1.1 concatenate.61
  456.9 1.1 concatenate.64
  (164 shorter events, 88.8 us)
Async XLA Ops:
  15.7 40.2 %all-to-all-start = ((bf16[128,2,384]{2,1,0:T(2,128)(2,1)}), bf16[128,2,384]{2,1,0:T(2,128)(2,1)S(1)}, u32[]{:S(2)}, u32[]{:S(2)}) async-start(bf16[128,2,384]{2,1,0:T(2,128)(2,1)} %reshape.477), calls=%async_computation | async-start | bytes 393216 | tf_op jit(solution)/shard_map/all_to_all | solution.py:69
  42.4 23.7 %copy-start.2 = (s32[4]{0:T(128)S(1)}, s32[4]{0:T(128)}, u32[]{:S(2)}) copy-start(s32[4]{0:T(128)} %param.15) | copy-start | bytes 52
  55.9 29.2 %copy-start.3 = (f32[32]{0:T(128)S(1)}, f32[32]{0:T(128)}, u32[]{:S(2)}) copy-start(f32[32]{0:T(128)} %param.10) | copy-start | bytes 388
  55.9 89.7 %all-to-all-start.1 = ((bf16[128,4,6,1024]{3,1,2,0:T(4,128)(2,1)}), bf16[128,4,6,1024]{3,1,2,0:T(4,128)(2,1)}, u32[]{:S(2)}, u32[]{:S(2)}) async-start(bf16[128,4,6,1024]{3,1,2,0:T(4,128)(2,1)} %copy.227), calls=%async_computation.1 | async-start | bytes 12582912 | tf_op jit(solution)/shard_map/all_to_all | solution.py:68
  66.1 162.2 %all-reduce.2.cloned.1.call-start = ((), (), s32[]{:S(2)}) async-start(), calls=%async_computation.2 | async-start | bytes 524288 | tf_op jit(solution)/shard_map/psum | solution.py:83
  158.0 117.3 %all-gather.6.cloned.1.call-start = ((), (), s32[]{:S(2)}) async-start(), calls=%async_computation.4 | async-start | bytes 2228224 | tf_op jit(solution)/shard_map/all_gather | solution.py:86
  160.3 129.0 %all-gather.4.cloned.1.call-start = ((), (), s32[]{:S(2)}) async-start(), calls=%async_computation.3 | async-start | bytes 4456448 | tf_op jit(solution)/shard_map/all_gather | solution.py:84
  292.0 1.3 copy-start
  293.3 42.2 %slice-start = ((s8[16777216]{0:T(1024)(128)(4,1)}), s8[4194304]{0:T(1024)(128)(4,1)S(1)}, s32[]{:S(2)}) async-start(s8[16777216]{0:T(1024)(128)(4,1)} %bitcast.543), calls=%async_computation.5 | async-start | bytes 8388608
  293.3 42.2 %slice-start.1 = ((s8[16777216]{0:T(1024)(128)(4,1)}), s8[4194304]{0:T(1024)(128)(4,1)S(1)}, s32[]{:S(2)}) async-start(s8[16777216]{0:T(1024)(128)(4,1)} %bitcast.543), calls=%async_computation.6 | async-start | bytes 8388608
  311.4 24.1 %slice-start.2 = ((s8[16777216]{0:T(1024)(128)(4,1)}), s8[4194304]{0:T(1024)(128)(4,1)S(1)}, s32[]{:S(2)}) async-start(s8[16777216]{0:T(1024)(128)(4,1)} %bitcast.543), calls=%async_computation.7 | async-start | bytes 8388608
  311.4 24.1 %slice-start.3 = ((s8[16777216]{0:T(1024)(128)(4,1)}), s8[4194304]{0:T(1024)(128)(4,1)S(1)}, s32[]{:S(2)}) async-start(s8[16777216]{0:T(1024)(128)(4,1)} %bitcast.543), calls=%async_computation.8 | async-start | bytes 8388608
  373.7 23.9 %copy-start.1 = (bf16[4,8,16,1024]{3,1,2,0:T(8,128)(2,1)S(1)}, bf16[4,8,16,1024]{3,1,2,0:T(8,128)(2,1)}, u32[]{:S(2)}) copy-start(bf16[4,8,16,1024]{3,1,2,0:T(8,128)(2,1)} %copy.297) | copy-start | bytes 3145732
Sparse Core Ops, SparseCore 0:
  158.1 70.0 all-reduce.1
Sparse Core Ops, SparseCore 1:
  161.4 49.9 all-gather.5
  228.3 60.8 all-gather.3
where the time goes:
time: 471 us; the launch traced here: 467 us
  matrix products  172 us (37%)
  waiting for transfers between devices  123 us (26%)
  local copies, waits for them, and re-layouts  121 us (26%)
  starting transfers between devices  22.1 us (5%)
  between operations  18.8 us (4%)
  other arithmetic  10.2 us (2%)
    dot_general x8, matrix products, per_device(): lax.dot_general(rolled, refs, (((1,), (1,)), ((), ())), preferred_element...  157 us
    unnamed x90, local copies, waits for them, and re-layouts  72.6 us
    all_to_all x1, waiting for transfers between devices, per_device(): got_img = lax.all_to_all(send_img, ('dom', 'cls'), 0, 0, tiled=True)  60.6 us
    psum x1, waiting for transfers between devices, per_device(): ref_chunks = lax.psum(jnp.stack(ref_chunks, axis=0), 'cls')  51.4 us
    another operation x3, local copies, waits for them, and re-layouts, per_device(): rolled = jnp.stack(views, axis=1).reshape(per_dev * count, pixels)  16.2 us
    all_to_all x1, starting transfers between devices, per_device(): got_wts = lax.all_to_all(send_wts, ('dom', 'cls'), 0, 0, tiled=True)  11.7 us
    all_gather x1, waiting for transfers between devices, per_device(): all_refs = lax.all_gather(ref_chunks, 'dom', axis=0, tiled=False)  10.8 us
    another operation x1, local copies, waits for them, and re-layouts, per_device(): jnp.stack(send_img, axis=2).reshape(doms * groups, STEPS, capacity, chunk)  10.3 us
  transfers between devices with their start and end apart: 5, of which 3 were waited for; matrix products, arithmetic and copies ran while one was open for 24% of the time, Pallas kernels for 0%

commit v1 on v0

--- a/solution.py
+++ b/solution.py
@@ -9,6 +9,10 @@
 ROT = 64
 STEPS = 4
 ASTEP = 2
+
+
+def _cut_pairs_all(local_x, dev_axis):
+    return jnp.sum(lax.all_gather(local_x, dev_axis), 0)
 
 
 def rotate_each(cube, shifts):
@@ -80,7 +84,7 @@
         piece = current.astype(jnp.bfloat16)
         piece = jnp.where(me_cls == owners[step], piece, jnp.zeros_like(piece))
         ref_chunks.append(piece)
-    ref_chunks = lax.psum(jnp.stack(ref_chunks, axis=0), "cls")
+    ref_chunks = _cut_pairs_all(jnp.stack(ref_chunks, axis=0), "cls")
     all_refs = lax.all_gather(ref_chunks, "dom", axis=0, tiled=False)
     all_refs = all_refs.transpose(1, 2, 0, 3).reshape(STEPS, per_group, pixels)
     final = lax.all_gather(current, "dom", axis=0, tiled=False)

time: 471 us -> 489 us (1.038)
  waiting for transfers between devices: 123 us -> 140 us
    psum x1 -> x0, waiting for transfers between devices: 51.4 us -> none  [per_device(): ref_chunks = lax.psum(jnp.stack(ref_chunks, axis=0), 'cls')]
    all_gather x1, waiting for transfers between devices: 10.8 us -> 54.6 us  [per_device(): all_refs = lax.all_gather(ref_chunks, 'dom', axis=0, tiled=False)]
    all_to_all x1, waiting for transfers between devices: 60.6 us -> 75 us  [per_device(): got_img = lax.all_to_all(send_img, ('dom', 'cls'), 0, 0, tiled=True)]
    all_gather x1, waiting for transfers between devices: 0.01 us -> 5.96 us  [per_device(): final = lax.all_gather(current, 'dom', axis=0, tiled=False)]
  transfers between devices with their start and end apart: 5 -> 5, of which waited for: 3 -> 4; matrix products, arithmetic and copies ran while one was open for 24% -> 24% of each run, Pallas kernels for 0% -> 0%
where the time goes in v1:
time: 489 us; the launch traced here: 485 us
  matrix products  172 us (35%)
  waiting for transfers between devices  140 us (29%)
  local copies, waits for them, and re-layouts  121 us (25%)
  starting transfers between devices  22.4 us (5%)
  between operations  17 us (3%)
  other arithmetic  13 us (3%)
    dot_general x8, matrix products, per_device(): lax.dot_general(rolled, refs, (((1,), (1,)), ((), ())), preferred_element...  157 us
    all_to_all x1, waiting for transfers between devices, per_device(): got_img = lax.all_to_all(send_img, ('dom', 'cls'), 0, 0, tiled=True)  75 us
    unnamed x90, local copies, waits for them, and re-layouts  72.6 us
    all_gather x1, waiting for transfers between devices, per_device(): all_refs = lax.all_gather(ref_chunks, 'dom', axis=0, tiled=False)  54.6 us
    another operation x3, local copies, waits for them, and re-layouts, per_device(): rolled = jnp.stack(views, axis=1).reshape(per_dev * count, pixels)  16.4 us
    all_to_all x1, starting transfers between devices, per_device(): got_wts = lax.all_to_all(send_wts, ('dom', 'cls'), 0, 0, tiled=True)  11.7 us
    another operation x1, local copies, waits for them, and re-layouts, per_device(): jnp.stack(send_img, axis=2).reshape(doms * groups, STEPS, capacity, chunk)  10.3 us
    all_to_all x1, starting transfers between devices, per_device(): got_img = lax.all_to_all(send_img, ('dom', 'cls'), 0, 0, tiled=True)  10.2 us
  transfers between devices with their start and end apart: 5, of which 4 were waited for; matrix products, arithmetic and copies ran while one was open for 24% of the time, Pallas kernels for 0%

profile of v1, /device:TPU:1, one launch (start us, length us, event | category | flops | bytes accessed | tf_op | source)
XLA Modules:
  0.0 485.2 jit_solution(6489368773196271245)
XLA Ops:
  13.6 1.3 reshape.479
  14.9 11.7 %all-to-all-start = ((bf16[128,2,384]{2,1,0:T(2,128)(2,1)}), bf16[128,2,384]{2,1,0:T(2,128)(2,1)S(1)}, u32[]{:S(2)}, u32[]{:S(2)}) async-start(bf16[128,2,384]{2,1,0:T(2,128)(2,1)} %reshape.479), calls=%async_computation | async-start | bytes 393216 | tf_op jit(solution)/shard_map/all_to_all | solution.py:73
  27.4 1.1 copy.342
  40.3 1.1 copy.421
  41.4 3.3 pad_maximum_fusion
  44.6 10.3 %copy.285 = bf16[128,4,6,1024]{3,1,2,0:T(4,128)(2,1)} copy(bf16[128,4,6,1024]{3,0,2,1:T(8,128)(2,1)} %pad_maximum_fusion) | data formatting | bytes 12582912 | tf_op jit(solution)/shard_map/stack | solution.py:70
  54.9 10.2 %all-to-all-start.1 = ((bf16[128,4,6,1024]{3,1,2,0:T(4,128)(2,1)}), bf16[128,4,6,1024]{3,1,2,0:T(4,128)(2,1)}, u32[]{:S(2)}, u32[]{:S(2)}) async-start(bf16[128,4,6,1024]{3,1,2,0:T(4,128)(2,1)} %copy.285), calls=%async_computation.1 | async-start | bytes 12582912 | tf_op jit(solution)/shard_map/all_to_all | solution.py:72
  69.7 75.0 %all-to-all-done.1 = bf16[128,4,6,1024]{3,1,2,0:T(4,128)(2,1)} async-done(((bf16[128,4,6,1024]{3,1,2,0:T(4,128)(2,1)}), bf16[128,4,6,1024]{3,1,2,0:T(4,128)(2,1)}, u32[]{:S(2)}, u32[]{:S(2)}) %all-to-all-start.1) | async-done | bytes 6291488 | tf_op jit(solution)/shard_map/all_to_all | solution.py:72
  144.7 9.7 %fusion.30 = f32[4,32,1024]{2,1,0:T(8,128)S(1)} fusion(bf16[128,4,6,1024]{3,1,2,0:T(4,128)(2,1)} %all-to-all-done.1, bf16[128,4,6,32]{3,1,2,0:T(4,128)(2,1)S(1)} %bitcast.550), kind=kOutput, calls=%fused_computation.44 | convolution fusion | flops 201326592 | bytes 7012352 | tf_op jit(solution)/shard_map/dot_general | solution.py:74
  190.4 4.4 all-gather.7.cloned.1.call-done
  194.8 2.7 reduce_sum.62
  198.6 14.3 %copy.267 = bf16[16,32,128,128]{3,2,1,0:T(8,128)(2,1)} copy(bf16[16,32,128,128]{3,2,0,1:T(8,128)(2,1)} %fusion.74) | data formatting | bytes 33554432 | tf_op jit(solution)/shard_map/stack | solution.py:102
  244.8 6.0 %all-gather.11.cloned.1.call-done = f32[512,1024]{1,0:T(8,128)} async-done(((f32[32,1024]{1,0:T(8,128)}), f32[512,1024]{1,0:T(8,128)}) %all-gather.11.cloned.1.call-update) | async-done | bytes 2097168 | tf_op jit(solution)/shard_map/all_gather | solution.py:90
  250.7 3.2 copy.341
  253.9 54.6 %all-gather.9.cloned.1.call-done = bf16[64,32,1024]{2,1,0:T(8,128)(2,1)} async-done(((bf16[4,32,1024]{2,1,0:T(8,128)(2,1)}), bf16[64,32,1024]{2,1,0:T(8,128)(2,1)}) %all-gather.9.cloned.1.call-update) | async-done | bytes 4194320 | tf_op jit(solution)/shard_map/all_gather | solution.py:88
  308.4 2.6 fusion.172
  311.1 1.2 copy.356
  312.5 18.1 %fusion = f32[512,32]{1,0:T(8,128)} fusion(bf16[32,16384]{1,0:T(8,128)(2,1)S(1)} %bitcast.576, bf16[64,8,128,128]{3,2,1,0:T(8,128)(2,1)} %bitcast.218), kind=kOutput, calls=%fused_computation.4 | convolution fusion | flops 536870912 | bytes 17891328 | tf_op jit(solution)/shard_map/dot_general | solution.py:103
  330.6 24.1 %fusion.2 = f32[512,32]{1,0:T(8,128)} fusion(bf16[32,16384]{1,0:T(8,128)(2,1)} %bitcast.578, bf16[64,8,128,128]{3,2,1,0:T(8,128)(2,1)} %bitcast.218), kind=kOutput, calls=%fused_computation.6 | convolution fusion | flops 536870912 | bytes 17891328 | tf_op jit(solution)/shard_map/dot_general | solution.py:103
  354.7 18.4 %fusion.8 = f32[512,32]{1,0:T(8,128)S(1)} fusion(bf16[32,16384]{1,0:T(8,128)(2,1)} %bitcast.577, bf16[64,8,128,128]{3,2,1,0:T(8,128)(2,1)S(1)} %bitcast.546), kind=kOutput, calls=%fused_computation.12 | convolution fusion | flops 536870912 | bytes 17891328 | tf_op jit(solution)/shard_map/dot_general | solution.py:103
  373.1 18.8 %fusion.10 = f32[512,32]{1,0:T(8,128)S(1)} fusion(bf16[32,16384]{1,0:T(8,128)(2,1)} %bitcast.579, bf16[64,8,128,128]{3,2,1,0:T(8,128)(2,1)S(1)} %bitcast.547), kind=kOutput, calls=%fused_computation.14 | convolution fusion | flops 536870912 | bytes 17891328 | tf_op jit(solution)/shard_map/dot_general | solution.py:103
  391.9 1.1 copy.355
  392.9 23.9 %fusion.4 = f32[512,32]{1,0:T(8,128)} fusion(bf16[32,16384]{1,0:T(8,128)(2,1)} %bitcast.582, bf16[64,8,128,128]{3,2,1,0:T(8,128)(2,1)} %bitcast.218), kind=kOutput, calls=%fused_computation.8 | convolution fusion | flops 536870912 | bytes 17891328 | tf_op jit(solution)/shard_map/dot_general | solution.py:103
  416.9 18.2 %fusion.12 = f32[512,32]{1,0:T(8,128)} fusion(bf16[32,16384]{1,0:T(8,128)(2,1)S(1)} %bitcast.583, bf16[64,8,128,128]{3,2,1,0:T(8,128)(2,1)S(1)} %bitcast.548), kind=kOutput, calls=%fused_computation.16 | convolution fusion | flops 536870912 | bytes 17891328 | tf_op jit(solution)/shard_map/dot_general | solution.py:103
  435.2 17.6 %fusion.6 = f32[512,32]{1,0:T(8,128)} fusion(bf16[32,16384]{1,0:T(8,128)(2,1)S(1)} %bitcast.580, bf16[64,8,128,128]{3,2,1,0:T(8,128)(2,1)} %bitcast.218), kind=kOutput, calls=%fused_computation.10 | convolution fusion | flops 536870912 | bytes 17891328 | tf_op jit(solution)/shard_map/dot_general | solution.py:103
  452.8 17.9 %fusion.14 = f32[512,32]{1,0:T(8,128)} fusion(bf16[32,16384]{1,0:T(8,128)(2,1)S(1)} %bitcast.581, bf16[64,8,128,128]{3,2,1,0:T(8,128)(2,1)S(1)} %bitcast.549), kind=kOutput, calls=%fused_computation.18 | convolution fusion | flops 536870912 | bytes 17891328 | tf_op jit(solution)/shard_map/dot_general | solution.py:103
  470.7 1.1 concatenate.71
  471.7 1.1 concatenate.68
  472.8 1.1 concatenate.62
  473.9 1.1 concatenate.65
  475.0 1.1 concatenate.61
  476.1 1.1 concatenate.64
  (165 shorter events, 91.1 us)
Async XLA Ops:
  14.9 40.1 %all-to-all-start = ((bf16[128,2,384]{2,1,0:T(2,128)(2,1)}), bf16[128,2,384]{2,1,0:T(2,128)(2,1)S(1)}, u32[]{:S(2)}, u32[]{:S(2)}) async-start(bf16[128,2,384]{2,1,0:T(2,128)(2,1)} %reshape.479), calls=%async_computation | async-start | bytes 393216 | tf_op jit(solution)/shard_map/all_to_all | solution.py:73
  41.3 23.8 %copy-start.2 = (s32[4]{0:T(128)S(1)}, s32[4]{0:T(128)}, u32[]{:S(2)}) copy-start(s32[4]{0:T(128)} %param.15) | copy-start | bytes 52
  44.6 25.0 %copy-start.3 = (f32[32]{0:T(128)S(1)}, f32[32]{0:T(128)}, u32[]{:S(2)}) copy-start(f32[32]{0:T(128)} %param.10) | copy-start | bytes 388
  54.9 89.8 %all-to-all-start.1 = ((bf16[128,4,6,1024]{3,1,2,0:T(4,128)(2,1)}), bf16[128,4,6,1024]{3,1,2,0:T(4,128)(2,1)}, u32[]{:S(2)}, u32[]{:S(2)}) async-start(bf16[128,4,6,1024]{3,1,2,0:T(4,128)(2,1)} %copy.285), calls=%async_computation.1 | async-start | bytes 12582912 | tf_op jit(solution)/shard_map/all_to_all | solution.py:72
  65.1 129.7 %all-gather.7.cloned.1.call-start = ((), (), s32[]{:S(2)}) async-start(), calls=%async_computation.2 | async-start | bytes 2359296 | tf_op jit(solution)/shard_map/all_gather | solution.py:15
  157.0 93.7 %all-gather.11.cloned.1.call-start = ((), (), s32[]{:S(2)}) async-start(), calls=%async_computation.4 | async-start | bytes 2228224 | tf_op jit(solution)/shard_map/all_gather | solution.py:90
  173.8 134.6 %all-gather.9.cloned.1.call-start = ((), (), s32[]{:S(2)}) async-start(), calls=%async_computation.3 | async-start | bytes 4456448 | tf_op jit(solution)/shard_map/all_gather | solution.py:88
  311.1 1.3 copy-start
  312.5 42.2 %slice-start = ((s8[16777216]{0:T(1024)(128)(4,1)}), s8[4194304]{0:T(1024)(128)(4,1)S(1)}, s32[]{:S(2)}) async-start(s8[16777216]{0:T(1024)(128)(4,1)} %bitcast.544), calls=%async_computation.5 | async-start | bytes 8388608
  312.5 42.2 %slice-start.1 = ((s8[16777216]{0:T(1024)(128)(4,1)}), s8[4194304]{0:T(1024)(128)(4,1)S(1)}, s32[]{:S(2)}) async-start(s8[16777216]{0:T(1024)(128)(4,1)} %bitcast.544), calls=%async_computation.6 | async-start | bytes 8388608
  330.6 24.1 %slice-start.2 = ((s8[16777216]{0:T(1024)(128)(4,1)}), s8[4194304]{0:T(1024)(128)(4,1)S(1)}, s32[]{:S(2)}) async-start(s8[16777216]{0:T(1024)(128)(4,1)} %bitcast.544), calls=%async_computation.7 | async-start | bytes 8388608
  330.6 24.1 %slice-start.3 = ((s8[16777216]{0:T(1024)(128)(4,1)}), s8[4194304]{0:T(1024)(128)(4,1)S(1)}, s32[]{:S(2)}) async-start(s8[16777216]{0:T(1024)(128)(4,1)} %bitcast.544), calls=%async_computation.8 | async-start | bytes 8388608
  392.9 23.9 %copy-start.1 = (bf16[4,8,16,1024]{3,1,2,0:T(8,128)(2,1)S(1)}, bf16[4,8,16,1024]{3,1,2,0:T(8,128)(2,1)}, u32[]{:S(2)}) copy-start(bf16[4,8,16,1024]{3,1,2,0:T(8,128)(2,1)} %copy.355) | copy-start | bytes 3145732
Sparse Core Ops, SparseCore 0:
  157.1 37.6 all-gather.6
  197.8 52.8 all-gather.10
  253.7 54.6 all-gather.8
